TPU v7x, 32 devices: a whole 2x2x4 slice. The times are simulated.
32 devices in a mesh: dp: 4 (over x, core), tensor: 8 (over z, y).
Axes of the slice: x: 2, y: 2, z: 4, core: 2. Of those that a mesh axis runs over, the one named last changes fastest.
Arguments:
- grad: bfloat16 [4, 576, 6144], P('dp', 'tensor'), as said below
- momentum: float32 [4, 576, 6144], P('dp', 'tensor'), may hold values from -6 to 6
- owner: int32 [4], replicated, may hold values from 0 to 3, each once
Outputs:
- update: bfloat16 [4, 576, 6144], P(None, 'tensor')
- new_momentum: float32 [4, 576, 6144], P('dp', 'tensor')
Inputs may be any that keep to these rules, and one draw needn't show every extreme that they name: owner names each matrix 0 to 3 exactly once. `grad`: gradient entries are finite; every matrix has full rank.
All inputs are finite; a program needn't handle non-finite values.
Results may differ from a plain program's by a relative error of at most 0.0013.
The roundings to bfloat16 on the way count: a program that leaves them out, or rounds other values in their place, can miss the bound.
Values may be sent and summed in bfloat16 or wider, within the bound.
No kernel may reach another device: no remote copies, remote signals or barrier semaphores. Data moves between devices by JAX's collectives and lax.ppermute only.
A program may use at most 64 MiB of HBM per device.

v0:
```python
import math
import jax
import jax.numpy as jnp
from jax import lax
from jax.sharding import PartitionSpec as P

M = 576
N = 6144
ITERS = 2
coef_a = 3.4445
coef_b = -4.775
coef_c = 2.0315
decay = 0.95
eps = 1e-07


def per_device(grad, momentum, owner):
    new_momentum = decay * momentum + grad.astype(jnp.float32)
    direction = grad.astype(jnp.float32) + decay * new_momentum
    total = lax.psum(jnp.sum(direction * direction), "tensor")
    rows_here = (direction[0] / (jnp.sqrt(total) + eps)).astype(jnp.bfloat16)
    columns = lax.all_to_all(rows_here, "tensor", split_axis=1, concat_axis=0, tiled=True)
    for step in range(ITERS):
        gram = lax.psum(
            jnp.dot(columns, columns.T, preferred_element_type=jnp.float32), "tensor"
        ).astype(jnp.bfloat16)
        square = jnp.dot(gram, gram, preferred_element_type=jnp.float32)
        poly = (coef_b * gram.astype(jnp.float32) + coef_c * square).astype(jnp.bfloat16)
        applied = jnp.dot(poly, columns, preferred_element_type=jnp.float32)
        columns = (coef_a * columns.astype(jnp.float32) + applied).astype(jnp.bfloat16)
    factor = 0.2 * math.sqrt(max(M, N))
    back_rows = lax.all_to_all(columns, "tensor", split_axis=0, concat_axis=1, tiled=True)
    scaled = (factor * back_rows.astype(jnp.float32)).astype(jnp.bfloat16)
    every_slot = lax.all_gather(scaled[None], "dp", axis=0, tiled=True)
    matrix_ids = jnp.arange(every_slot.shape[0], dtype=jnp.int32)
    selector = (owner[None, :] == matrix_ids[:, None]).astype(jnp.bfloat16)
    update = jnp.einsum(
        "mg,grn->mrn", selector, every_slot, preferred_element_type=jnp.float32
    ).astype(jnp.bfloat16)
    return (update, new_momentum)


def solution(mesh):
    in_specs = (P("dp", "tensor", None), P("dp", "tensor", None), P())
    out_specs = (P(None, "tensor", None), P("dp", "tensor", None))
    return jax.shard_map(
        per_device, mesh=mesh, in_specs=in_specs, out_specs=out_specs, check_vma=False
    )
```

profile of v0, /device:TPU:0, one launch (start us, length us, event | category | flops | bytes accessed | tf_op | source)
XLA Modules:
  0.0 286.8 jit_solution(11792428714496908145)
XLA Ops:
  7.2 0.0 copy-start.1
  7.2 0.0 all-gather.2.cloned.1.call-start
  7.2 2.9 %multiply_reduce_fusion = (f32[]{:T(128)}, f32[1,72,6144]{2,1,0:T(8,128)S(1)}) fusion(bf16[1,72,6144]{2,1,0:T(8,128)(2,1)} %param.3, f32[1,72,6144]{2,1,0:T(8,128)} %param.4), kind=kLoop, calls=%fused_computation.8 | loop fusion | flops 3096575 | bytes 4423684 | tf_op jit(solution)/shard_map/reduce_sum | solution.py:20
  10.1 0.0 copy-start
  10.1 23.8 %psum.21 = f32[]{:T(128)} all-reduce(f32[]{:T(128)} %get-tuple-element.8), channel_id=1, replica_groups=mesh['dp'=4,'tensor'=8] {'tensor'}, use_global_device_ids=true, to_apply=%region_1.0 | all-reduce | flops 1 | bytes 8 | tf_op jit(solution)/shard_map/psum | solution.py:20
  34.6 0.0 copy-done.1
  34.6 0.3 divide_convert_fusion
  34.8 0.0 copy-done
  34.9 0.2 copy.16
  35.0 0.2 copy.12
  35.2 21.7 %all_to_all.29 = bf16[72,8,768]{2,0,1:T(8,128)(2,1)S(1)} all-to-all(bf16[72,8,768]{2,0,1:T(8,128)(2,1)S(1)} %copy.12), channel_id=1, replica_groups=mesh['dp'=4,'tensor'=8] {'tensor'}, dimensions={1} | all-to-all | bytes 1769472 | tf_op jit(solution)/shard_map/all_to_all | solution.py:22
  56.9 0.9 fusion.17
  57.7 79.9 %all-reduce.2 = bf16[576,576]{1,0:T(8,128)(2,1)S(1)} all-reduce(f32[576,576]{1,0:T(8,128)S(1)} %fusion.17), channel_id=1, replica_groups=mesh['dp'=4,'tensor'=8] {'tensor'}, use_global_device_ids=true, to_apply=%region_2.0 | all-reduce | flops 331776 | bytes 1990656 | tf_op jit(solution)/shard_map/psum | solution.py:24
  137.6 1.6 add_convert_fusion.1
  139.3 0.0 copy-start.3
  139.3 0.9 copy-done.3
  140.2 0.9 fusion.18
  141.1 0.0 copy-start.4
  141.1 78.1 %all-reduce.3 = bf16[576,576]{1,0:T(8,128)(2,1)S(1)} all-reduce(f32[576,576]{1,0:T(8,128)S(1)} %fusion.18), channel_id=1, replica_groups=mesh['dp'=4,'tensor'=8] {'tensor'}, use_global_device_ids=true, to_apply=%region_3.0 | all-reduce | flops 331776 | bytes 1990656 | tf_op jit(solution)/shard_map/psum | solution.py:24
  219.2 0.0 copy-done.4
  219.2 1.6 add_convert_fusion
  220.8 18.7 %all_to_all.30 = bf16[8,72,768]{2,1,0:T(8,128)(2,1)S(1)} all-to-all(bf16[8,72,768]{2,1,0:T(8,128)(2,1)S(1)} %bitcast.26), channel_id=1, replica_groups=mesh['dp'=4,'tensor'=8] {'tensor'}, dimensions={0} | all-to-all | bytes 1769472 | tf_op jit(solution)/shard_map/all_to_all | solution.py:32
  239.6 0.2 fusion.1
  239.7 0.2 copy.13
  239.9 0.0 copy-start.2
  239.9 1.3 convert_element_type.89
  241.2 0.0 all-gather.2.cloned.1.call-update
  241.2 28.5 %all-gather.2.cloned.1.call-done = bf16[4,72,6144]{2,1,0:T(8,128)(2,1)} async-done(((bf16[1,72,6144]{2,1,0:T(8,128)(2,1)}), bf16[4,72,6144]{2,1,0:T(8,128)(2,1)}) %all-gather.2.cloned.1.call-update) | async-done | bytes 3538960 | tf_op jit(solution)/shard_map/all_gather | solution.py:34
  269.7 0.0 copy-done.2
  269.7 6.5 %convolution_convert_fusion = bf16[4,72,6144]{2,0,1:T(4,128)(2,1)S(1)} fusion(bf16[4,72,6144]{2,1,0:T(8,128)(2,1)} %all-gather.2.cloned.1.call-done, s32[4]{0:T(128)S(1)} %copy-done.2), kind=kOutput, calls=%fused_computation | convolution fusion | flops 15925264 | bytes 7077904 | tf_op jit(solution)/shard_map/mg,grn->mrn/dot_general | solution.py:37
  276.2 3.7 %copy.15 = bf16[4,72,6144]{2,1,0:T(8,128)(2,1)} copy(bf16[4,72,6144]{2,0,1:T(4,128)(2,1)S(1)} %convolution_convert_fusion) | data formatting | bytes 7077888
Async XLA Ops:
  7.2 27.4 %copy-start.1 = (bf16[1,72,6144]{2,1,0:T(8,128)(2,1)S(1)}, bf16[1,72,6144]{2,1,0:T(8,128)(2,1)}, u32[]{:S(2)}) copy-start(bf16[1,72,6144]{2,1,0:T(8,128)(2,1)} %param.3) | copy-start | bytes 2654212
  7.2 262.5 %all-gather.2.cloned.1.call-start = ((), (), s32[]{:S(2)}) async-start(), calls=%async_computation.2 | async-start | bytes 4423680 | tf_op jit(solution)/shard_map/all_gather | solution.py:34
  10.1 24.7 %copy-start = (f32[1,72,6144]{2,1,0:T(8,128)}, f32[1,72,6144]{2,1,0:T(8,128)S(1)}, u32[]{:S(2)}) copy-start(f32[1,72,6144]{2,1,0:T(8,128)S(1)} %get-tuple-element.9) | copy-start | bytes 5308420
  139.3 0.9 copy-start.3
  141.1 78.1 %copy-start.4 = (bf16[576,768]{1,0:T(8,128)(2,1)S(1)}, bf16[576,768]{1,0:T(8,128)(2,1)}, u32[]{:S(2)}) copy-start(bf16[576,768]{1,0:T(8,128)(2,1)} %copy-done.3) | copy-start | bytes 2654212
  239.9 29.8 %copy-start.2 = (s32[4]{0:T(128)S(1)}, s32[4]{0:T(128)}, u32[]{:S(2)}) copy-start(s32[4]{0:T(128)} %param.5) | copy-start | bytes 52
Sparse Core Ops, SparseCore 0:
  241.3 28.2 all-gather.1
where the time goes:
time: 287 us
  blocking collectives  222 us (77%)
  waiting for transfers between devices  28.5 us (10%)
  between operations  14.8 us (5%)
  matrix products  11.6 us (4%)
  local copies, waits for them, and re-layouts  6.44 us (2%)
  other arithmetic  3.29 us (1%)
    psum x2, blocking collectives, per_device(): lax.psum(jnp.dot(columns, columns.T, preferred_element_type=jnp.float32),...  158 us
    all_gather x1, waiting for transfers between devices, per_device(): every_slot = lax.all_gather(scaled[None], 'dp', axis=0, tiled=True)  28.5 us
    psum x1, blocking collectives, per_device(): total = lax.psum(jnp.sum(direction * direction), 'tensor')  23.8 us
    all_to_all x1, blocking collectives, per_device(): lax.all_to_all(rows_here, 'tensor', split_axis=1, concat_axis=0, tiled=True)  21.7 us
    all_to_all x1, blocking collectives, per_device(): lax.all_to_all(columns, 'tensor', split_axis=0, concat_axis=1, tiled=True)  18.7 us
    dot_general x1, matrix products, per_device(): jnp.einsum('mg,grn->mrn', selector, every_slot, preferred_element_type=jn...  6.52 us
  transfers between devices with their start and end apart: 1, of which 1 were waited for; matrix products, arithmetic and copies ran while one was open for 0% of the time, Pallas kernels for 0%

commit v1 on v0

--- a/solution.py
+++ b/solution.py
@@ -31,7 +31,23 @@
     factor = 0.2 * math.sqrt(max(M, N))
     back_rows = lax.all_to_all(columns, "tensor", split_axis=0, concat_axis=1, tiled=True)
     scaled = (factor * back_rows.astype(jnp.float32)).astype(jnp.bfloat16)
-    every_slot = lax.all_gather(scaled[None], "dp", axis=0, tiled=True)
+
+    def show_cells(frame_in):
+        comm_axis = "dp"
+        axis_n = lax.psum(1, comm_axis)
+        heap = [(hop_no, (hop_no + 1) % axis_n) for hop_no in range(axis_n)]
+        sides = [(hop_no, (hop_no - 1) % axis_n) for hop_no in range(axis_n)]
+        val2, v1 = ([frame_in], [frame_in])
+        for _ in range(axis_n // 2):
+            val2.append(lax.ppermute(val2[-1], axis_name=comm_axis, perm=heap))
+        for _ in range((axis_n - 1) // 2):
+            v1.append(lax.ppermute(v1[-1], comm_axis, sides))
+        base_arr = jnp.concatenate([*val2[::-1], *v1[1:]], 0)
+        return jnp.roll(
+            base_arr, (lax.axis_index(comm_axis) - axis_n // 2) * frame_in.shape[0], axis=0
+        )
+
+    every_slot = show_cells(scaled[None])
     matrix_ids = jnp.arange(every_slot.shape[0], dtype=jnp.int32)
     selector = (owner[None, :] == matrix_ids[:, None]).astype(jnp.bfloat16)
     update = jnp.einsum(

time: 287 us -> 330 us (1.15); the launches traced: 287 us -> 325 us
  local copies, waits for them, and re-layouts: 6.44 us -> 62.1 us
  between operations: 14.8 us -> 1.47 us
  waiting for transfers between devices: 28.5 us -> 23.8 us
    concatenate x0 -> x1, local copies, waits for them, and re-layouts: none -> 43 us  [show_cells(): jnp.roll(base_arr, (lax.axis_index(comm_axis) - axis_n // 2) * frame_in.s...]
    all_gather x1 -> x0, waiting for transfers between devices: 28.5 us -> none  [per_device(): every_slot = lax.all_gather(scaled[None], 'dp', axis=0, tiled=True)]
    ppermute x0 -> x3, waiting for transfers between devices: none -> 23.8 us  [the longest x2 23.8 us: show_cells(): val2.append(lax.ppermute(val2[-1], axis_name=comm_axis, perm=heap))]
    ppermute x0 -> x3, local copies, waits for them, and re-layouts: none -> 10.1 us  [the longest x2 6.27 us: show_cells(): val2.append(lax.ppermute(val2[-1], axis_name=comm_axis, perm=heap))]
  transfers between devices with their start and end apart: 1 -> 3, of which waited for: 1 -> 2; matrix products, arithmetic and copies ran while one was open for 0% -> 3% of each run, Pallas kernels for 0% -> 0%
where the time goes in v1:
time: 330 us; the launch traced here: 325 us
  blocking collectives  222 us (67%)
  local copies, waits for them, and re-layouts  62.1 us (19%)
  waiting for transfers between devices  23.8 us (7%)
  matrix products  10.2 us (3%)
    psum x2, blocking collectives, per_device(): lax.psum(jnp.dot(columns, columns.T, preferred_element_type=jnp.float32),...  160 us
    concatenate x1, local copies, waits for them, and re-layouts, show_cells(): jnp.roll(base_arr, (lax.axis_index(comm_axis) - axis_n // 2) * frame_in.s...  43 us
    psum x1, blocking collectives, per_device(): total = lax.psum(jnp.sum(direction * direction), 'tensor')  23.8 us
    ppermute x2, waiting for transfers between devices, show_cells(): val2.append(lax.ppermute(val2[-1], axis_name=comm_axis, perm=heap))  23.8 us
    all_to_all x1, blocking collectives, per_device(): lax.all_to_all(rows_here, 'tensor', split_axis=1, concat_axis=0, tiled=True)  21.7 us
    all_to_all x1, blocking collectives, per_device(): lax.all_to_all(columns, 'tensor', split_axis=0, concat_axis=1, tiled=True)  17.1 us
  transfers between devices with their start and end apart: 3, of which 2 were waited for; matrix products, arithmetic and copies ran while one was open for 3% of the time, Pallas kernels for 0%

profile of v1, /device:TPU:0, one launch (start us, length us, event | category | flops | bytes accessed | tf_op | source)
XLA Modules:
  0.0 324.6 jit_solution(15238831439382099425)
XLA Ops:
  0.6 2.9 multiply_reduce_fusion
  3.5 23.8 %psum.21 = f32[]{:T(128)} all-reduce(f32[]{:T(128)} %get-tuple-element.8), channel_id=1, replica_groups=mesh['dp'=4,'tensor'=8] {'tensor'}, use_global_device_ids=true, to_apply=%region_1.0 | all-reduce | flops 1 | bytes 8 | tf_op jit(solution)/shard_map/psum | solution.py:20
  28.0 0.3 divide_convert_fusion
  28.3 0.2 copy.26
  28.4 0.2 copy.15
  28.6 21.7 %all_to_all.29 = bf16[72,8,768]{2,0,1:T(8,128)(2,1)S(1)} all-to-all(bf16[72,8,768]{2,0,1:T(8,128)(2,1)S(1)} %copy.15), channel_id=1, replica_groups=mesh['dp'=4,'tensor'=8] {'tensor'}, dimensions={1} | all-to-all | bytes 1769472 | tf_op jit(solution)/shard_map/all_to_all | solution.py:22
  50.3 0.9 fusion.18
  51.2 80.3 %all-reduce.2 = bf16[576,576]{1,0:T(8,128)(2,1)S(1)} all-reduce(f32[576,576]{1,0:T(8,128)S(1)} %fusion.18), channel_id=1, replica_groups=mesh['dp'=4,'tensor'=8] {'tensor'}, use_global_device_ids=true, to_apply=%region_2.0 | all-reduce | flops 331776 | bytes 1990656 | tf_op jit(solution)/shard_map/psum | solution.py:24
  131.5 1.6 add_convert_fusion.1
  133.1 0.0 copy-start.3
  133.1 0.9 copy-done.3
  134.0 0.9 fusion.19
  134.9 0.0 copy-start.4
  134.9 79.2 %all-reduce.3 = bf16[576,576]{1,0:T(8,128)(2,1)S(1)} all-reduce(f32[576,576]{1,0:T(8,128)S(1)} %fusion.19), channel_id=1, replica_groups=mesh['dp'=4,'tensor'=8] {'tensor'}, use_global_device_ids=true, to_apply=%region_3.0 | all-reduce | flops 331776 | bytes 1990656 | tf_op jit(solution)/shard_map/psum | solution.py:24
  214.1 1.6 add_convert_fusion
  215.8 17.1 %all_to_all.30 = bf16[8,72,768]{2,1,0:T(8,128)(2,1)S(1)} all-to-all(bf16[8,72,768]{2,1,0:T(8,128)(2,1)S(1)} %bitcast.26), channel_id=1, replica_groups=mesh['dp'=4,'tensor'=8] {'tensor'}, dimensions={0} | all-to-all | bytes 1769472 | tf_op jit(solution)/shard_map/all_to_all | solution.py:32
  232.9 0.2 fusion.1
  233.0 0.2 copy.16
  233.2 1.3 convert_element_type.89
  234.5 0.0 collective-permute-start
  234.5 1.7 collective-permute-start.2
  236.3 19.9 %collective-permute-done = bf16[1,72,6144]{2,1,0:T(8,128)(2,1)} collective-permute-done((bf16[1,72,6144]{2,1,0:T(8,128)(2,1)}, bf16[1,72,6144]{2,1,0:T(8,128)(2,1)}, u32[]{:S(2)}, u32[]{:S(2)}) %collective-permute-start) | collective-permute-done | bytes 884768 | tf_op jit(solution)/shard_map/ppermute | solution.py:42
  256.1 0.0 collective-permute-start.1
  256.1 2.5 copy.19
  258.7 2.5 copy.18
  261.2 0.0 collective-permute-done.2
  261.2 3.8 %copy.20 = bf16[1,72,6144]{2,0,1:T(2,128)(2,1)} copy(bf16[1,72,6144]{2,1,0:T(8,128)(2,1)} %collective-permute-done.2) | data formatting | bytes 1769472 | tf_op jit(solution)/shard_map/ppermute | solution.py:44
  265.1 3.9 %collective-permute-done.1 = bf16[1,72,6144]{2,1,0:T(8,128)(2,1)} collective-permute-done((bf16[1,72,6144]{2,1,0:T(8,128)(2,1)}, bf16[1,72,6144]{2,1,0:T(8,128)(2,1)}, u32[]{:S(2)}, u32[]{:S(2)}) %collective-permute-start.1) | collective-permute-done | bytes 884768 | tf_op jit(solution)/shard_map/ppermute | solution.py:42
  268.9 3.7 %copy.17 = bf16[1,72,6144]{2,0,1:T(2,128)(2,1)} copy(bf16[1,72,6144]{2,1,0:T(8,128)(2,1)} %collective-permute-done.1) | data formatting | bytes 1769472 | tf_op jit(solution)/shard_map/ppermute | solution.py:42
  272.7 43.0 %concatenate.6 = bf16[8,72,6144]{2,0,1:T(8,128)(2,1)} concatenate(bf16[1,72,6144]{2,0,1:T(2,128)(2,1)} %copy.17, bf16[1,72,6144]{2,0,1:T(2,128)(2,1)S(1)} %copy.18, bf16[1,72,6144]{2,0,1:T(2,128)(2,1)S(1)} %copy.19, bf16[1,72,6144]{2,0,1:T(2,128)(2,1)} %copy.20, bf16[1,72,6144]{2,0,1:T(2,128)(2,1)} %copy.17, bf16[1,72,6144]{2,0,1:T(2,128)(2,1)S(1)} %copy.18, ...), dimensions={0} | concatenate | bytes 14155776 | tf_op jit(solution)/shard_map/jit(_roll_dynamic)/concatenate | solution.py:46
  315.7 5.2 %convolution_convert_fusion = bf16[4,72,6144]{2,0,1:T(4,128)(2,1)S(1)} fusion(bf16[8,72,6144]{2,0,1:T(8,128)(2,1)} %concatenate.6, s32[]{:T(128)S(6)} %select_n.14, s32[4]{0:T(128)S(1)} %copy-done.2), kind=kOutput, calls=%fused_computation | convolution fusion | flops 15925264 | bytes 7077908 | tf_op jit(solution)/shard_map/mg,grn->mrn/dot_general | solution.py:53
  320.9 3.7 %copy.25 = bf16[4,72,6144]{2,1,0:T(8,128)(2,1)} copy(bf16[4,72,6144]{2,0,1:T(4,128)(2,1)S(1)} %convolution_convert_fusion) | data formatting | bytes 7077888
  (7 shorter events, 0.0 us)
Async XLA Ops:
  0.6 27.4 %copy-start.1 = (bf16[1,72,6144]{2,1,0:T(8,128)(2,1)S(1)}, bf16[1,72,6144]{2,1,0:T(8,128)(2,1)}, u32[]{:S(2)}) copy-start(bf16[1,72,6144]{2,1,0:T(8,128)(2,1)} %param.3) | copy-start | bytes 2654212
  3.5 24.7 %copy-start = (f32[1,72,6144]{2,1,0:T(8,128)}, f32[1,72,6144]{2,1,0:T(8,128)S(1)}, u32[]{:S(2)}) copy-start(f32[1,72,6144]{2,1,0:T(8,128)S(1)} %get-tuple-element.9) | copy-start | bytes 5308420
  133.1 0.9 copy-start.3
  134.9 79.2 %copy-start.4 = (bf16[576,768]{1,0:T(8,128)(2,1)S(1)}, bf16[576,768]{1,0:T(8,128)(2,1)}, u32[]{:S(2)}) copy-start(bf16[576,768]{1,0:T(8,128)(2,1)} %copy-done.3) | copy-start | bytes 2654212
  234.5 21.6 %collective-permute-start = (bf16[1,72,6144]{2,1,0:T(8,128)(2,1)}, bf16[1,72,6144]{2,1,0:T(8,128)(2,1)}, u32[]{:S(2)}, u32[]{:S(2)}) collective-permute-start(bf16[1,72,6144]{2,1,0:T(8,128)(2,1)} %convert_element_type.89), channel_id=1, source_target_pairs={{0,8},{8,16},{16,24},{24,0},{1,9},{9,17},{17,25},{25,1},{2,10},{10... | collective-permute-start | bytes 2654216 | tf_op jit(solution)/shard_map/ppermute | solution.py:42
  234.5 26.7 %collective-permute-start.2 = (bf16[1,72,6144]{2,1,0:T(8,128)(2,1)}, bf16[1,72,6144]{2,1,0:T(8,128)(2,1)}, u32[]{:S(2)}, u32[]{:S(2)}) collective-permute-start(bf16[1,72,6144]{2,1,0:T(8,128)(2,1)} %convert_element_type.89), channel_id=1, source_target_pairs={{0,24},{8,0},{16,8},{24,16},{1,25},{9,1},{17,9},{25,17},{2,26},{10... | collective-permute-start | bytes 2654216 | tf_op jit(solution)/shard_map/ppermute | solution.py:44
  256.1 12.8 %collective-permute-start.1 = (bf16[1,72,6144]{2,1,0:T(8,128)(2,1)}, bf16[1,72,6144]{2,1,0:T(8,128)(2,1)}, u32[]{:S(2)}, u32[]{:S(2)}) collective-permute-start(bf16[1,72,6144]{2,1,0:T(8,128)(2,1)} %collective-permute-done), channel_id=1, source_target_pairs={{0,8},{8,16},{16,24},{24,0},{1,9},{9,17},{17,25},{25,1},{2,10},{10... | collective-permute-start | bytes 2654216 | tf_op jit(solution)/shard_map/ppermute | solution.py:42
  272.7 43.0 %copy-start.2 = (s32[4]{0:T(128)S(1)}, s32[4]{0:T(128)}, u32[]{:S(2)}) copy-start(s32[4]{0:T(128)} %param.5) | copy-start | bytes 52
